TPU v7x, 32 devices: a whole 2x2x4 slice. The times are simulated.
32 devices in a mesh: bucket: 8 (over z, x), rel: 4 (over y, core).
Axes of the slice: x: 2, y: 2, z: 4, core: 2. Of those that a mesh axis runs over, the one named last changes fastest.
Arguments:
- left_rows: float32 [8192, 512], P(('bucket', 'rel')), may hold values from -1.2 to 1.2
- left_state: float32 [8192], P(('bucket', 'rel')), may hold values from 1e-06 to 0.0001
- right_rows: float32 [8192, 512], P(('bucket', 'rel')), may hold values from -1.2 to 1.2
- right_state: float32 [8192], P(('bucket', 'rel')), may hold values from 1e-06 to 0.0001
- relations: bfloat16 [4, 512, 512], P('rel'), may hold values from -0.25 to 0.25
- fetch_ids: int32 [8, 4, 4], P('bucket', 'rel'), may hold values from 0 to 3
- edge_left: int32 [8, 4, 2, 512], P('bucket', 'rel'), may hold values from 0 to 255
- edge_right: int32 [8, 4, 2, 512], P('bucket', 'rel'), may hold values from 0 to 255
- edge_slot: int32 [8, 4, 2, 512], P('bucket', 'rel'), may hold values from 0 to 1
- edge_weight: int32 [8, 4, 2, 512], P('bucket', 'rel'), may hold values from 1 to 4
- matching: int32 [1], replicated, may hold values from 1 to 7
Outputs:
- left_out: float32 [8192, 512], P(('bucket', 'rel'))
- left_state_out: float32 [8192], P(('bucket', 'rel'))
- right_out: float32 [8192, 512], P(('bucket', 'rel'))
- right_state_out: float32 [8192], P(('bucket', 'rel'))
- rel_grad: float32 [4, 512, 512], P('rel')
Inputs may be any that keep to these rules, and one draw needn't show every extreme that they name: Bucket b is paired with bucket b XOR matching.
All inputs are finite; a program needn't handle non-finite values.
Results may differ from a plain program's by a relative error of at most 0.0015.
The roundings to bfloat16 on the way count: a program that leaves them out, or rounds other values in their place, can miss the bound.
Values may be sent and summed in bfloat16 or wider, within the bound.
No kernel may reach another device: no remote copies, remote signals or barrier semaphores. Data moves between devices by JAX's collectives and lax.ppermute only.
A program may use at most 64 MiB of HBM per device.

v0:
```python
import jax
import jax.numpy as jnp
from jax import lax
from jax.sharding import PartitionSpec as P

learn_rate = 0.1


def edge_targets(edge_left, edge_right, edge_slot, edge_weight, block_len):
    table = jnp.zeros((2, block_len, block_len), jnp.float32)
    table = table.at[edge_slot, edge_left, edge_right].add(edge_weight.astype(jnp.float32))
    return [table[0], table[1]]


def adagrad(table, state, gradient):
    state_new = state + jnp.mean(gradient * gradient, axis=1)
    return (table - learn_rate * gradient / jnp.sqrt(state_new)[:, None], state_new)


def one_round(
    left_block,
    left_st,
    right_block,
    right_st,
    rel_pair,
    edge_left,
    edge_right,
    edge_slot,
    edge_weight,
):
    block_len = left_block.shape[0]
    left_half = left_block.astype(jnp.bfloat16)
    right_half = right_block.astype(jnp.bfloat16)
    targets = edge_targets(edge_left, edge_right, edge_slot, edge_weight, block_len)
    grad_left = jnp.zeros(left_block.shape, jnp.float32)
    grad_right = jnp.zeros(right_block.shape, jnp.float32)
    rel_grads = []
    for slot_index in range(2):
        matrix = rel_pair[slot_index]
        projected = jnp.dot(left_half, matrix, preferred_element_type=jnp.float32).astype(
            jnp.bfloat16
        )
        scores = jnp.dot(projected, right_half.T, preferred_element_type=jnp.float32)
        score_grad = ((jax.nn.sigmoid(scores) - targets[slot_index]) / block_len).astype(
            jnp.bfloat16
        )
        carried = jnp.dot(score_grad, right_half, preferred_element_type=jnp.float32).astype(
            jnp.bfloat16
        )
        grad_left = grad_left + jnp.dot(carried, matrix.T, preferred_element_type=jnp.float32)
        grad_right = grad_right + jnp.dot(
            score_grad.T, projected, preferred_element_type=jnp.float32
        )
        rel_grads.append(jnp.dot(left_half.T, carried, preferred_element_type=jnp.float32))
    left_new, left_st_new = adagrad(left_block, left_st, grad_left)
    right_new, right_st_new = adagrad(right_block, right_st, grad_right)
    return (left_new, left_st_new, right_new, right_st_new, rel_grads)


def partner_blocks(row_block, state_block, switch):
    block_len = row_block.shape[0]
    width = row_block.shape[1]
    partner = jnp.bitwise_xor(lax.axis_index("bucket"), switch)
    portion = (
        lax.all_gather(row_block, "bucket", axis=0, tiled=True),
        lax.all_gather(state_block, "bucket", axis=0, tiled=True),
    )
    block_count = portion[0].shape[0] // block_len
    owners = jnp.arange(block_count, dtype=jnp.int32)
    chosen = owners == partner
    rows_part = portion[0].reshape(block_count, block_len, width)
    states_part = portion[1].reshape(block_count, block_len)
    rows_new = jnp.sum(jnp.where(chosen[:, None, None], rows_part, jnp.float32(0.0)), axis=0)
    states_new = jnp.sum(jnp.where(chosen[:, None], states_part, jnp.float32(0.0)), axis=0)
    return (rows_new, states_new)


def reduce_gradients(gradients, rel_ids, rel_total, width):
    stacked = jnp.stack(gradients)
    own_rows = rel_total // lax.axis_size("rel") * width
    rel_count_piece = own_rows * lax.axis_size("rel") // width
    rel_list = jnp.arange(rel_count_piece, dtype=jnp.int32)
    weights = (rel_ids[:, None] == rel_list[None, :]).astype(jnp.float32)
    term = jnp.einsum("sk,sde->kde", weights, stacked, precision=lax.Precision.HIGHEST)
    partial_sum = lax.psum_scatter(
        term.reshape(rel_count_piece * width, width), "rel", scatter_dimension=0, tiled=True
    )
    return lax.psum(partial_sum, "bucket")


def on_device(
    left_rows,
    left_state,
    right_rows,
    right_state,
    relations,
    fetch_ids,
    edge_left,
    edge_right,
    edge_slot,
    edge_weight,
    matching,
):
    width = relations.shape[1]
    rel_table = lax.all_gather(relations, "rel", axis=0, tiled=True)
    rel_total = rel_table.shape[0]
    rel_ids = fetch_ids[0, 0]
    switch = matching[0]
    table_left, state_left = (left_rows, left_state)
    row_block, state_block = (right_rows, right_state)
    gradients = []
    for round_index in range(2):
        rel_pair = jnp.take(rel_table, rel_ids[2 * round_index : 2 * round_index + 2], axis=0)
        table_left, state_left, row_block, state_block, rel_grads = one_round(
            table_left,
            state_left,
            row_block,
            state_block,
            rel_pair,
            edge_left[0, 0, round_index],
            edge_right[0, 0, round_index],
            edge_slot[0, 0, round_index],
            edge_weight[0, 0, round_index],
        )
        gradients.extend(rel_grads)
        if round_index == 0:
            row_block, state_block = partner_blocks(row_block, state_block, switch)
    owned = reduce_gradients(gradients, rel_ids, rel_total, width)
    return (table_left, state_left, row_block, state_block, owned.reshape(-1, width, width))


def solution(mesh):
    in_specs = (
        P(("bucket", "rel"), None),
        P(("bucket", "rel")),
        P(("bucket", "rel"), None),
        P(("bucket", "rel")),
        P("rel", None, None),
        P("bucket", "rel", None),
        P("bucket", "rel", None, None),
        P("bucket", "rel", None, None),
        P("bucket", "rel", None, None),
        P("bucket", "rel", None, None),
        P(),
    )
    out_specs = (
        P(("bucket", "rel"), None),
        P(("bucket", "rel")),
        P(("bucket", "rel"), None),
        P(("bucket", "rel")),
        P("rel", None, None),
    )
    return jax.shard_map(
        on_device, mesh=mesh, in_specs=in_specs, out_specs=out_specs, check_vma=False
    )
```

profile of v0, /device:TPU:0, one launch (start us, length us, event | category | flops | bytes accessed | tf_op | source)
XLA Modules:
  0.0 281.4 jit_solution(3566939604815437510)
XLA Ops:
  8.0 1.1 convert_element_type.65
  9.0 1.1 convert_element_type.63
  11.7 31.3 %scatter_fusion = f32[2,256,256]{2,1,0:T(8,128)S(1)} fusion(f32[2,256,256]{2,1,0:T(8,128)S(1)} %broadcast.145.clone, s32[512]{0:T(512)S(1)} %bitcast.126, f32[512]{0:T(512)S(1)} %bitcast.131), kind=kCustom, calls=%fused_computation.2 | custom fusion | flops 512 | bytes 12288 | tf_op jit(solution)/shard_map/scatter-add | solution.py:11
  43.7 2.2 gather_fusion
  50.5 31.3 %scatter_fusion.1 = f32[2,256,256]{2,1,0:T(8,128)S(1)} fusion(f32[2,256,256]{2,1,0:T(8,128)S(1)} %broadcast.145.clone.1, s32[512]{0:T(512)S(1)} %bitcast.125, f32[512]{0:T(512)S(1)} %bitcast.130), kind=kCustom, calls=%fused_computation.3 | custom fusion | flops 512 | bytes 12288 | tf_op jit(solution)/shard_map/scatter-add | solution.py:11
  82.3 3.2 %gather_fusion.1 = bf16[2,512,512]{2,1,0:T(8,128)(2,1)} fusion(bf16[4,512,512]{2,1,0:T(8,128)(2,1)} %all-gather.4.cloned.1.call-done, s32[1024]{0:T(1024)S(1)} %get-tuple-element.30), kind=kCustom, calls=%fused_computation.1.clone | custom fusion | bytes 2097160 | tf_op jit(solution)/shard_map/jit(_take)/gather | solution.py:113
  85.8 1.3 convolution_bitcast_fusion.2
  87.3 1.3 convolution_bitcast_fusion.3
  91.1 34.1 %all-gather.6.cloned.1.call-done = f32[2048,512]{1,0:T(8,128)} async-done(((f32[256,512]{1,0:T(8,128)}), f32[2048,512]{1,0:T(8,128)}) %all-gather.6.cloned.1.call-update) | async-done | bytes 4194320 | tf_op jit(solution)/shard_map/all_gather | solution.py:65
  125.2 2.9 %select_reduce_fusion = f32[256,512]{1,0:T(8,128)S(1)} fusion(f32[8,256,512]{2,1,0:T(8,128)} %bitcast.128, pred[8]{0:T(512)(128)(4,1)S(1)} %copy-done.14), kind=kLoop, calls=%fused_computation.5 | loop fusion | flops 1966080 | bytes 4718600 | tf_op jit(solution)/shard_map/reduce_sum | solution.py:73
  130.3 2.4 pad_maximum_fusion
  132.7 5.5 %copy.25 = f32[4,512,512]{2,0,1:T(4,128)} copy(f32[4,512,512]{1,2,0:T(8,128)} %pad_maximum_fusion) | data formatting | bytes 8388608 | tf_op jit(solution)/shard_map/stack | solution.py:79
  138.2 6.2 %fusion.32 = f32[4,512,512]{2,0,1:T(4,128)S(1)} fusion(f32[4,512,512]{2,0,1:T(4,128)} %copy.25, s32[4]{0:T(128)S(1)} %bitcast.132), kind=kOutput, calls=%fused_computation.98 | convolution fusion | flops 50331664 | bytes 8388624 | tf_op jit(solution)/shard_map/sk,sde->kde/dot_general | solution.py:84
  144.4 3.2 %copy.26 = f32[4,512,512]{2,1,0:T(8,128)} copy(f32[4,512,512]{2,0,1:T(4,128)S(1)} %fusion.32) | data formatting | bytes 8388608 | tf_op jit(solution)/shard_map/sk,sde->kde/dot_general | solution.py:84
  148.3 18.1 %all-gather = f32[8,1,256]{2,1,0:T(1,128)S(1)} all-gather(f32[1,1,256]{2,1,0:T(1,128)S(1)} %bitcast.133), channel_id=1, replica_groups=mesh['bucket'=8,'rel'=4] {'bucket'}, dimensions={0}, use_global_device_ids=true | all-gather | bytes 9216 | tf_op jit(solution)/shard_map/all_gather | solution.py:66
  166.5 1.2 fusion.41
  167.7 1.1 fusion.25
  168.9 2.0 multiply_reduce_fusion
  170.9 20.1 %reduce-scatter.2.cloned.1.call-done = f32[512,512]{1,0:T(8,128)} async-done(((f32[2048,512]{1,0:T(8,128)}), f32[512,512]{1,0:T(8,128)}) %reduce-scatter.2.cloned.1.call-update) | async-done | bytes 1048592 | tf_op jit(solution)/shard_map/reduce_scatter | solution.py:85
  191.6 1.5 multiply_reduce_fusion.1
  193.6 2.0 divide_subtract_fusion
  195.5 1.0 divide_subtract_fusion.1
  196.6 76.1 %all-reduce.2.cloned.1.call-done = f32[1,512,512]{2,1,0:T(8,128)} async-done(((f32[1,512,512]{2,1,0:T(8,128)}), f32[1,512,512]{2,1,0:T(8,128)}) %all-reduce.2.cloned.1.call-update) | async-done | bytes 1048592 | tf_op jit(solution)/shard_map/psum | solution.py:88
  272.6 2.3 copy.35
  (80 shorter events, 14.3 us)
Async XLA Ops:
  7.2 35.9 %copy-start.11 = (s32[1,1,4]{2,1,0:T(1,128)S(1)}, s32[1,1,4]{2,1,0:T(1,128)}, u32[]{:S(2)}) copy-start(s32[1,1,4]{2,1,0:T(1,128)} %param.18) | copy-start | bytes 52
  7.2 36.5 %all-gather.4.cloned.1.call-start = ((), (), s32[]{:S(2)}) async-start(), calls=%async_computation.1 | async-start | bytes 2621440 | tf_op jit(solution)/shard_map/all_gather | solution.py:105
  7.9 117.3 %all-gather.6.cloned.1.call-start = ((), (), s32[]{:S(2)}) async-start(), calls=%async_computation.2 | async-start | bytes 4718592 | tf_op jit(solution)/shard_map/all_gather | solution.py:65
  46.1 2.0 copy-start.17
  46.1 2.5 copy-start.6
  49.6 141.4 %reduce-scatter.2.cloned.1.call-start = ((), (), s32[]{:S(2)}) async-start(), calls=%async_computation.3 | async-start | bytes 5242880 | tf_op jit(solution)/shard_map/reduce_scatter | solution.py:85
  85.5 3.9 %copy-start.12 = (f32[256]{0:T(256)S(1)}, f32[256]{0:T(256)}, u32[]{:S(2)}) copy-start(f32[256]{0:T(256)} %param.14) | copy-start | bytes 3076
  85.5 3.9 %copy-start = (f32[256,512]{1,0:T(8,128)S(1)}, f32[256,512]{1,0:T(8,128)}, u32[]{:S(2)}) copy-start(f32[256,512]{1,0:T(8,128)} %param.13) | copy-start | bytes 1572868
  85.7 3.8 %copy-start.1 = (bf16[2,512,512]{2,1,0:T(8,128)(2,1)S(1)}, bf16[2,512,512]{2,1,0:T(8,128)(2,1)}, u32[]{:S(2)}) copy-start(bf16[2,512,512]{2,1,0:T(8,128)(2,1)} %gather_fusion.1) | copy-start | bytes 3145732
  85.8 3.8 %copy-start.16 = (pred[2]{0:T(512)(128)(4,1)S(1)}, pred[2]{0:T(512)(128)(4,1)}, u32[]{:S(2)}) copy-start(pred[2]{0:T(512)(128)(4,1)} %get-tuple-element.12) | copy-start | bytes 10
  88.6 36.6 %copy-start.14 = (pred[8]{0:T(512)(128)(4,1)S(1)}, pred[8]{0:T(512)(128)(4,1)}, u32[]{:S(2)}) copy-start(pred[8]{0:T(512)(128)(4,1)} %iota_compare_fusion.1) | copy-start | bytes 28
  89.5 35.7 %copy-start.4 = (bf16[256,512]{1,0:T(8,128)(2,1)}, bf16[256,512]{1,0:T(8,128)(2,1)S(1)}, u32[]{:S(2)}) copy-start(bf16[256,512]{1,0:T(8,128)(2,1)S(1)} %fusion.36) | copy-start | bytes 786436
  90.0 38.1 %copy-start.9 = (bf16[256,512]{1,0:T(8,128)(2,1)}, bf16[256,512]{1,0:T(8,128)(2,1)S(1)}, u32[]{:S(2)}) copy-start(bf16[256,512]{1,0:T(8,128)(2,1)S(1)} %convolution_convert_fusion.1) | copy-start | bytes 786436
  125.2 3.5 %copy-start.10 = (bf16[256,512]{1,0:T(8,128)(2,1)S(1)}, bf16[256,512]{1,0:T(8,128)(2,1)}, u32[]{:S(2)}) copy-start(bf16[256,512]{1,0:T(8,128)(2,1)} %convolution_convert_fusion.3) | copy-start | bytes 786436
  125.2 4.4 %copy-start.5 = (bf16[256,512]{1,0:T(8,128)(2,1)S(1)}, bf16[256,512]{1,0:T(8,128)(2,1)}, u32[]{:S(2)}) copy-start(bf16[256,512]{1,0:T(8,128)(2,1)} %copy-done.4) | copy-start | bytes 786436
  128.1 2.3 copy-start.2
  128.1 2.3 copy-start.3
  129.0 0.7 copy-start.7
  147.7 0.7 copy-start.13
  147.7 18.8 %copy-start.15 = (pred[8]{0:T(512)(128)(4,1)S(1)}, pred[8]{0:T(512)(128)(4,1)}, u32[]{:S(2)}) copy-start(pred[8]{0:T(512)(128)(4,1)} %iota_compare_fusion.1) | copy-start | bytes 28
  147.7 18.9 %copy-start.8 = (bf16[256,256]{1,0:T(8,128)(2,1)S(1)}, bf16[256,256]{1,0:T(8,128)(2,1)}, u32[]{:S(2)}) copy-start(bf16[256,256]{1,0:T(8,128)(2,1)} %copy-done.7) | copy-start | bytes 393220
  147.7 124.9 %all-reduce.2.cloned.1.call-start = ((), (), s32[]{:S(2)}) async-start(), calls=%async_computation.4 | async-start | bytes 2097152 | tf_op jit(solution)/shard_map/psum | solution.py:88
Sparse Core Ops, SparseCore 0:
  9.5 25.2 all-gather.3
  49.7 75.4 all-gather.5
  147.8 43.1 reduce-scatter.1
  194.3 78.2 all-reduce.1
where the time goes:
time: 282 us; the launch traced here: 281 us
  waiting for transfers between devices  131 us (46%)
  other arithmetic  79 us (28%)
  matrix products  20.7 us (7%)
  blocking collectives  18.1 us (6%)
  local copies, waits for them, and re-layouts  17.5 us (6%)
  between operations  14.8 us (5%)
    psum x1, waiting for transfers between devices, reduce_gradients(): return lax.psum(partial_sum, 'bucket')  76.1 us
    scatter-add x2, other arithmetic, edge_targets(): table.at[edge_slot, edge_left, edge_right]  62.7 us
    all_gather x1, waiting for transfers between devices, partner_blocks(): lax.all_gather(row_block, 'bucket', axis=0, tiled=True)  34.1 us
    reduce_scatter x1, waiting for transfers between devices, reduce_gradients(): lax.psum_scatter(term.reshape(rel_count_piece * width, width), 'rel', sca...  20.1 us
    all_gather x1, blocking collectives, partner_blocks(): lax.all_gather(state_block, 'bucket', axis=0, tiled=True)  18.1 us
    dot_general x1, matrix products, reduce_gradients(): jnp.einsum('sk,sde->kde', weights, stacked, precision=lax.Precision.HIGHEST)  6.2 us
  transfers between devices with their start and end apart: 4, of which 3 were waited for; matrix products, arithmetic and copies ran while one was open for 31% of the time, Pallas kernels for 0%

commit v1 on v0

--- a/solution.py
+++ b/solution.py
@@ -61,8 +61,18 @@
     block_len = row_block.shape[0]
     width = row_block.shape[1]
     partner = jnp.bitwise_xor(lax.axis_index("bucket"), switch)
+
+    def _convert_patches(x_part):
+        next_value = lax.all_to_all(
+            jnp.stack(lax.axis_size("bucket") * [x_part], axis=0),
+            concat_axis=0,
+            axis_name="bucket",
+            split_axis=0,
+        )
+        return jnp.concatenate(next_value, axis=0)
+
     portion = (
-        lax.all_gather(row_block, "bucket", axis=0, tiled=True),
+        _convert_patches(row_block),
         lax.all_gather(state_block, "bucket", axis=0, tiled=True),
     )
     block_count = portion[0].shape[0] // block_len

time: 282 us -> 309 us (1.096)
  waiting for transfers between devices: 131 us -> 149 us
  starting transfers between devices: 0.34 us -> 7.53 us
    all_to_all x0 -> x1, waiting for transfers between devices: none -> 51.7 us  [_convert_patches(): lax.all_to_all(jnp.stack(lax.axis_size('bucket') * [x_part], axis=0), con...]
    all_gather x1 -> x0, waiting for transfers between devices: 34.1 us -> none  [partner_blocks(): lax.all_gather(row_block, 'bucket', axis=0, tiled=True)]
    all_to_all x0 -> x1, starting transfers between devices: none -> 7.23 us  [_convert_patches(): lax.all_to_all(jnp.stack(lax.axis_size('bucket') * [x_part], axis=0), con...]
  transfers between devices with their start and end apart: 4 -> 4, of which waited for: 3 -> 3; matrix products, arithmetic and copies ran while one was open for 31% -> 28% of each run, Pallas kernels for 0% -> 0%
where the time goes in v1:
time: 309 us; the launch traced here: 308 us
  waiting for transfers between devices  149 us (48%)
  other arithmetic  78.4 us (25%)
  matrix products  20 us (6%)
  local copies, waits for them, and re-layouts  19.6 us (6%)
  blocking collectives  18.6 us (6%)
  between operations  14.8 us (5%)
  starting transfers between devices  7.53 us (2%)
    psum x1, waiting for transfers between devices, reduce_gradients(): return lax.psum(partial_sum, 'bucket')  76.5 us
    scatter-add x2, other arithmetic, edge_targets(): table.at[edge_slot, edge_left, edge_right]  62.7 us
    all_to_all x1, waiting for transfers between devices, _convert_patches(): lax.all_to_all(jnp.stack(lax.axis_size('bucket') * [x_part], axis=0), con...  51.7 us
    reduce_scatter x1, waiting for transfers between devices, reduce_gradients(): lax.psum_scatter(term.reshape(rel_count_piece * width, width), 'rel', sca...  20.2 us
    all_gather x1, blocking collectives, partner_blocks(): lax.all_gather(state_block, 'bucket', axis=0, tiled=True)  18.6 us
    all_to_all x1, starting transfers between devices, _convert_patches(): lax.all_to_all(jnp.stack(lax.axis_size('bucket') * [x_part], axis=0), con...  7.23 us
    dot_general x1, matrix products, reduce_gradients(): jnp.einsum('sk,sde->kde', weights, stacked, precision=lax.Precision.HIGHEST)  6.2 us
  transfers between devices with their start and end apart: 4, of which 3 were waited for; matrix products, arithmetic and copies ran while one was open for 28% of the time, Pallas kernels for 0%

profile of v1, /device:TPU:0, one launch (start us, length us, event | category | flops | bytes accessed | tf_op | source)
XLA Modules:
  0.0 308.2 jit_solution(6568396244047299165)
XLA Ops:
  7.9 1.1 convert_element_type.63
  11.7 31.3 %scatter_fusion = f32[2,256,256]{2,1,0:T(8,128)S(1)} fusion(f32[2,256,256]{2,1,0:T(8,128)S(1)} %broadcast.147.clone, s32[512]{0:T(512)S(1)} %bitcast.125, f32[512]{0:T(512)S(1)} %bitcast.129), kind=kCustom, calls=%fused_computation.2 | custom fusion | flops 512 | bytes 12288 | tf_op jit(solution)/shard_map/scatter-add | solution.py:11
  43.6 2.2 gather_fusion
  48.7 2.5 stack.12
  51.2 7.2 %all-to-all-start = ((f32[8,256,512]{2,1,0:T(8,128)}), f32[8,256,512]{2,1,0:T(8,128)}, u32[]{:S(2)}, u32[]{:S(2)}) async-start(f32[8,256,512]{2,1,0:T(8,128)} %stack.12), calls=%async_computation | async-start | bytes 8388608 | tf_op jit(solution)/shard_map/all_to_all | solution.py:66
  59.4 31.3 %scatter_fusion.1 = f32[2,256,256]{2,1,0:T(8,128)S(1)} fusion(f32[2,256,256]{2,1,0:T(8,128)S(1)} %broadcast.147.clone.1, s32[512]{0:T(512)S(1)} %bitcast.124, f32[512]{0:T(512)S(1)} %bitcast.128), kind=kCustom, calls=%fused_computation.3 | custom fusion | flops 512 | bytes 12288 | tf_op jit(solution)/shard_map/scatter-add | solution.py:11
  91.3 3.2 %gather_fusion.1 = bf16[2,512,512]{2,1,0:T(8,128)(2,1)} fusion(bf16[4,512,512]{2,1,0:T(8,128)(2,1)} %all-gather.3.cloned.1.call-done, s32[1024]{0:T(1024)S(1)} %get-tuple-element.30), kind=kCustom, calls=%fused_computation.1.clone | custom fusion | bytes 2097160 | tf_op jit(solution)/shard_map/jit(_take)/gather | solution.py:123
  94.7 1.4 convolution_bitcast_fusion.2
  96.3 1.3 convolution_bitcast_fusion.3
  100.0 51.7 %all-to-all-done = f32[8,256,512]{2,1,0:T(8,128)} async-done(((f32[8,256,512]{2,1,0:T(8,128)}), f32[8,256,512]{2,1,0:T(8,128)}, u32[]{:S(2)}, u32[]{:S(2)}) %all-to-all-start) | async-done | bytes 4194336 | tf_op jit(solution)/shard_map/all_to_all | solution.py:66
  151.8 2.9 select_reduce_fusion
  156.5 2.4 pad_maximum_fusion
  158.9 5.5 %copy.29 = f32[4,512,512]{2,0,1:T(4,128)} copy(f32[4,512,512]{1,2,0:T(8,128)} %pad_maximum_fusion) | data formatting | bytes 8388608 | tf_op jit(solution)/shard_map/stack | solution.py:89
  164.4 6.2 %fusion.32 = f32[4,512,512]{2,0,1:T(4,128)S(1)} fusion(f32[4,512,512]{2,0,1:T(4,128)} %copy.29, s32[4]{0:T(128)S(1)} %bitcast.130), kind=kOutput, calls=%fused_computation.98 | convolution fusion | flops 50331664 | bytes 8388624 | tf_op jit(solution)/shard_map/sk,sde->kde/dot_general | solution.py:94
  170.6 3.2 %copy.30 = f32[4,512,512]{2,1,0:T(8,128)} copy(f32[4,512,512]{2,0,1:T(4,128)S(1)} %fusion.32) | data formatting | bytes 8388608 | tf_op jit(solution)/shard_map/sk,sde->kde/dot_general | solution.py:94
  174.5 18.6 %all-gather = f32[8,1,256]{2,1,0:T(1,128)S(1)} all-gather(f32[1,1,256]{2,1,0:T(1,128)S(1)} %bitcast.131), channel_id=1, replica_groups=mesh['bucket'=8,'rel'=4] {'bucket'}, dimensions={0}, use_global_device_ids=true | all-gather | bytes 9216 | tf_op jit(solution)/shard_map/all_gather | solution.py:76
  193.8 1.2 fusion.41
  195.0 1.1 fusion.25
  196.1 1.3 multiply_reduce_fusion
  197.4 20.2 %reduce-scatter.2.cloned.1.call-done = f32[512,512]{1,0:T(8,128)} async-done(((f32[2048,512]{1,0:T(8,128)}), f32[512,512]{1,0:T(8,128)}) %reduce-scatter.2.cloned.1.call-update) | async-done | bytes 1048592 | tf_op jit(solution)/shard_map/reduce_scatter | solution.py:95
  217.6 1.2 fusion.37
  218.9 1.5 multiply_reduce_fusion.1
  222.8 76.5 %all-reduce.2.cloned.1.call-done = f32[1,512,512]{2,1,0:T(8,128)} async-done(((f32[1,512,512]{2,1,0:T(8,128)}), f32[1,512,512]{2,1,0:T(8,128)}) %all-reduce.2.cloned.1.call-update) | async-done | bytes 1048592 | tf_op jit(solution)/shard_map/psum | solution.py:98
  299.4 2.3 copy.39
  (80 shorter events, 16.1 us)
Async XLA Ops:
  7.2 35.9 %copy-start.11 = (s32[1,1,4]{2,1,0:T(1,128)S(1)}, s32[1,1,4]{2,1,0:T(1,128)}, u32[]{:S(2)}) copy-start(s32[1,1,4]{2,1,0:T(1,128)} %param.18) | copy-start | bytes 52
  7.2 36.5 %all-gather.3.cloned.1.call-start = ((), (), s32[]{:S(2)}) async-start(), calls=%async_computation.2 | async-start | bytes 2621440 | tf_op jit(solution)/shard_map/all_gather | solution.py:115
  46.0 2.0 copy-start.17
  46.0 2.5 copy-start.6
  51.2 100.5 %all-to-all-start = ((f32[8,256,512]{2,1,0:T(8,128)}), f32[8,256,512]{2,1,0:T(8,128)}, u32[]{:S(2)}, u32[]{:S(2)}) async-start(f32[8,256,512]{2,1,0:T(8,128)} %stack.12), calls=%async_computation | async-start | bytes 8388608 | tf_op jit(solution)/shard_map/all_to_all | solution.py:66
  58.4 159.2 %reduce-scatter.2.cloned.1.call-start = ((), (), s32[]{:S(2)}) async-start(), calls=%async_computation.3 | async-start | bytes 5242880 | tf_op jit(solution)/shard_map/reduce_scatter | solution.py:95
  94.4 3.9 %copy-start.12 = (f32[256]{0:T(256)S(1)}, f32[256]{0:T(256)}, u32[]{:S(2)}) copy-start(f32[256]{0:T(256)} %param.14) | copy-start | bytes 3076
  94.4 3.9 %copy-start = (f32[256,512]{1,0:T(8,128)S(1)}, f32[256,512]{1,0:T(8,128)}, u32[]{:S(2)}) copy-start(f32[256,512]{1,0:T(8,128)} %param.13) | copy-start | bytes 1572868
  94.7 3.9 %copy-start.1 = (bf16[2,512,512]{2,1,0:T(8,128)(2,1)S(1)}, bf16[2,512,512]{2,1,0:T(8,128)(2,1)}, u32[]{:S(2)}) copy-start(bf16[2,512,512]{2,1,0:T(8,128)(2,1)} %gather_fusion.1) | copy-start | bytes 3145732
  94.7 3.9 %copy-start.16 = (pred[2]{0:T(512)(128)(4,1)S(1)}, pred[2]{0:T(512)(128)(4,1)}, u32[]{:S(2)}) copy-start(pred[2]{0:T(512)(128)(4,1)} %get-tuple-element.12) | copy-start | bytes 10
  97.6 54.1 %copy-start.14 = (pred[8]{0:T(512)(128)(4,1)S(1)}, pred[8]{0:T(512)(128)(4,1)}, u32[]{:S(2)}) copy-start(pred[8]{0:T(512)(128)(4,1)} %iota_compare_fusion.1) | copy-start | bytes 28
  98.5 1.5 copy-start.4
  99.0 55.7 %copy-start.10 = (bf16[256,512]{1,0:T(8,128)(2,1)}, bf16[256,512]{1,0:T(8,128)(2,1)S(1)}, u32[]{:S(2)}) copy-start(bf16[256,512]{1,0:T(8,128)(2,1)S(1)} %convolution_convert_fusion.3) | copy-start | bytes 786436
  151.7 3.5 %copy-start.9 = (bf16[256,512]{1,0:T(8,128)(2,1)S(1)}, bf16[256,512]{1,0:T(8,128)(2,1)}, u32[]{:S(2)}) copy-start(bf16[256,512]{1,0:T(8,128)(2,1)} %convolution_convert_fusion.1) | copy-start | bytes 786436
  151.8 4.0 %copy-start.5 = (bf16[256,512]{1,0:T(8,128)(2,1)S(1)}, bf16[256,512]{1,0:T(8,128)(2,1)}, u32[]{:S(2)}) copy-start(bf16[256,512]{1,0:T(8,128)(2,1)} %copy-done.4) | copy-start | bytes 786436
  154.6 1.9 copy-start.2
  154.6 1.9 copy-start.3
  155.0 0.8 copy-start.7
  173.8 0.7 copy-start.13
  173.8 19.3 %copy-start.15 = (pred[8]{0:T(512)(128)(4,1)S(1)}, pred[8]{0:T(512)(128)(4,1)}, u32[]{:S(2)}) copy-start(pred[8]{0:T(512)(128)(4,1)} %iota_compare_fusion.1) | copy-start | bytes 28
  173.8 19.9 %copy-start.8 = (bf16[256,256]{1,0:T(8,128)(2,1)S(1)}, bf16[256,256]{1,0:T(8,128)(2,1)}, u32[]{:S(2)}) copy-start(bf16[256,256]{1,0:T(8,128)(2,1)} %copy-done.7) | copy-start | bytes 393220
  173.9 125.5 %all-reduce.2.cloned.1.call-start = ((), (), s32[]{:S(2)}) async-start(), calls=%async_computation.4 | async-start | bytes 2097152 | tf_op jit(solution)/shard_map/psum | solution.py:98
Sparse Core Ops, SparseCore 0:
  9.5 25.2 all-gather.2
  174.0 43.5 reduce-scatter.1
  221.1 78.2 all-reduce.1
